TPU v7x, 256 devices: a whole 4x4x8 slice. The times are simulated.
256 devices in a mesh: row: 32 (over z, x), col: 8 (over y, core).
Axes of the slice: x: 4, y: 4, z: 8, core: 2. Of those that a mesh axis runs over, the one named last changes fastest.
Arguments:
- x_points: bfloat16 [32768, 64], P(('row', 'col')), may hold values from -6 to 6
- y_points: bfloat16 [65536, 64], P(('col', 'row')), may hold values from -6 to 6
- row_mass: bfloat16 [32768], P(('row', 'col')), may hold values from 1 to 30, as said below
- col_mass: bfloat16 [65536], P(('col', 'row')), may hold values from 1 to 30, as said below
- multipliers: bfloat16 [32768, 64], P(('row', 'col')), may hold values from -12 to 12
- col_potential: bfloat16 [65536], P(('col', 'row')), may hold values from -3 to 3
- basket: float32 [64], replicated, may hold values from 0.05 to 0.25
- damping: float32 [64], replicated, may hold values from 0.3 to 1.5
Outputs:
- row_potential: float32 [32768], P('row')
- col_potential_new: float32 [65536], P('col')
- multipliers_new: float32 [32768, 64], P(('row', 'col'))
Inputs may be any that keep to these rules, and one draw needn't show every extreme that they name: `row_mass`: weights rise along the points' order by up to a factor of three. `col_mass`: weights rise along the points' order by up to a factor of three.
All inputs are finite; a program needn't handle non-finite values.
Results may differ from a plain program's by a relative error of at most 0.0012.
Values may be sent and summed in bfloat16 or wider, within the bound.
No kernel may reach another device: no remote copies, remote signals or barrier semaphores. Data moves between devices by JAX's collectives and lax.ppermute only.
A program may use at most 64 MiB of HBM per device.

v0:
```python
import jax
import jax.numpy as jnp
from jax import lax
from jax.sharding import PartitionSpec as P

EPS = 0.5
KAPPA = 0.5
RIDGE = 1.0


def merge_lse(parts):
    top = jnp.max(parts, axis=0)
    return top + jnp.log(jnp.sum(jnp.exp(parts - top[None, :]), axis=0))


def on_device(x_points, y_points, row_mass, col_mass, multipliers, col_potential, basket, damping):
    width = x_points.shape[1]
    share = x_points.shape[0]
    x_pack = jnp.concatenate([x_points, multipliers, row_mass[:, None]], axis=1)
    x_rows_pack = lax.all_gather(x_pack, "col", axis=0, tiled=True)
    x_rows = x_rows_pack[:, :width]
    mult_rows = x_rows_pack[:, width : 2 * width]
    mass_rows = x_rows_pack[:, 2 * width]
    ny = y_points.shape[0]
    own_rmass = jnp.zeros((ny,), jnp.bfloat16).at[:share].set(row_mass)
    y_pack = jnp.concatenate(
        [y_points, col_potential[:, None], col_mass[:, None], own_rmass[:, None]], axis=1
    )
    y_cols_pack = lax.all_gather(y_pack, "row", axis=0, tiled=True)
    y_cols = y_cols_pack[:, :width]
    pot_cols = y_cols_pack[:, width].astype(jnp.float32)
    mass_cols = y_cols_pack[:, width + 1].astype(jnp.float32)
    rmass_part = jnp.sum(y_cols_pack[:, width + 2].astype(jnp.float32))
    xf = x_rows.astype(jnp.float32)
    hf = mult_rows.astype(jnp.float32)
    yf = y_cols.astype(jnp.float32)
    row_term2 = 2.0 * (-jnp.sum(hf * xf, axis=1) - KAPPA / width * jnp.sum(xf * xf, axis=1))
    row_basket2 = 2.0 * jnp.sum(xf * basket[None, :], axis=1)
    col_term2 = 2.0 * (-(KAPPA / width) * jnp.sum(yf * yf, axis=1))
    col_basket2 = 2.0 * jnp.sum(yf * basket[None, :], axis=1)
    q_aug = jnp.concatenate([mult_rows * 2, x_rows * (2.0 * KAPPA / width * 2.0)], axis=1)
    y_aug = jnp.concatenate([y_cols, y_cols], axis=1)
    features = jnp.concatenate([yf, yf * yf], axis=1).astype(jnp.bfloat16)
    row_weight = mass_rows.astype(jnp.float32)
    log_row = jnp.log(row_weight)
    log_col = jnp.log(mass_cols)
    nrows = x_rows.shape[0]
    block = min(128, nrows)
    count = nrows // block
    starts = jnp.arange(count, dtype=jnp.int32) * block

    def cut(arr, start):
        return lax.dynamic_slice_in_dim(arr, start, block, 0)

    def block_z(start, row_bias, col_bias):
        dots = jnp.dot(cut(q_aug, start), y_aug.T, preferred_element_type=jnp.float32)
        payoff = jnp.maximum(col_basket2[None, :] - cut(row_basket2, start)[:, None], 0.0)
        return dots + cut(row_bias, start)[:, None] + col_bias[None, :] + payoff

    gshift = col_term2 + pot_cols / EPS + log_col
    zero_rows = jnp.zeros((nrows,), jnp.float32)

    def row_pass(start):
        z = block_z(start, row_term2, gshift)
        top = jnp.max(z, axis=1)
        total = jnp.sum(jnp.exp(z - top[:, None]), axis=1)
        return top + jnp.log(total)

    row_local = lax.map(row_pass, starts).reshape(nrows)
    nu_part = jnp.sum(mass_cols)
    row_msg = jnp.concatenate([row_local, jnp.stack([nu_part, rmass_part])])
    row_all = lax.all_gather(row_msg, "col", axis=0)
    nu_total = jnp.sum(row_all[:, nrows])
    mu_total = jnp.sum(row_all[:, nrows + 1])
    log_nu_total = jnp.log(nu_total)
    row_potential = -EPS * (merge_lse(row_all[:, :nrows]) - log_nu_total)
    fshift = row_term2 + row_potential / EPS + log_row
    zero_cols = jnp.zeros_like(gshift)

    def col_pass(start):
        z = block_z(start, fshift, col_term2)
        top = jnp.max(z, axis=0)
        total = jnp.sum(jnp.exp(z - top[None, :]), axis=0)
        return (top, total)

    col_tops, col_totals = lax.map(col_pass, starts)
    col_top = jnp.max(col_tops, axis=0)
    col_total = jnp.sum(col_totals * jnp.exp(col_tops - col_top[None, :]), axis=0)
    col_local = col_top + jnp.log(col_total)
    col_all = lax.all_gather(col_local, "row", axis=0)
    col_potential_new = -EPS * (merge_lse(col_all) - jnp.log(mu_total))
    gq = col_term2 + col_potential_new / EPS + log_col - log_nu_total
    fq = row_term2 + row_potential / EPS

    def moment_pass(start):
        plan = jnp.exp(block_z(start, fq, gq)).astype(jnp.bfloat16)
        both = jnp.dot(plan, features, preferred_element_type=jnp.float32)
        mass = jnp.sum(plan.astype(jnp.float32), axis=1)
        return jnp.concatenate([both, mass[:, None]], axis=1)

    both = lax.map(moment_pass, starts).reshape(nrows, 2 * width + 1)
    own = lax.psum_scatter(both, "col", scatter_dimension=0, tiled=True)
    first = own[:, :width]
    second = own[:, width : 2 * width]
    own_mass = own[:, 2 * width]
    xo = x_points.astype(jnp.float32)
    grad = first - xo * own_mass[:, None]
    curv = (second - 2.0 * xo * first + xo * xo * own_mass[:, None]) / EPS + RIDGE
    multipliers_new = multipliers.astype(jnp.float32) - damping[None, :] * grad / curv
    return (row_potential, col_potential_new, multipliers_new)


def solution(mesh):
    placed = (
        P(("row", "col"), None),
        P(("col", "row"), None),
        P(("row", "col")),
        P(("col", "row")),
        P(("row", "col"), None),
        P(("col", "row")),
        P(),
        P(),
    )
    return jax.shard_map(
        on_device,
        mesh=mesh,
        in_specs=placed,
        out_specs=(P("row"), P("col"), P(("row", "col"), None)),
        check_vma=False,
    )
```

profile of v0, /device:TPU:4, one launch (start us, length us, event | category | flops | bytes accessed | tf_op | source)
XLA Modules:
  0.0 432.3 jit_solution(2858686389016648679)
XLA Ops:
  14.9 13.6 %all_gather.16 = bf16[1024,129]{1,0:T(8,128)(2,1)S(1)} all-gather(bf16[128,129]{1,0:T(8,128)(2,1)S(1)} %pad_maximum_fusion.3), channel_id=1, replica_groups=mesh['row'=32,'col'=8] {'col'}, dimensions={0}, use_global_device_ids=true | all-gather | bytes 297216 | tf_op jit(solution)/shard_map/all_gather | solution.py:20
  30.3 60.3 %all-gather.5.cloned.1.call-done = bf16[8192,67]{1,0:T(8,128)(2,1)} async-done(((bf16[256,67]{1,0:T(8,128)(2,1)}), bf16[8192,67]{1,0:T(8,128)(2,1)}) %all-gather.5.cloned.1.call-update) | async-done | bytes 1097744 | tf_op jit(solution)/shard_map/all_gather | solution.py:29
  90.7 4.0 fusion.16
  94.7 3.4 pad_maximum_fusion.1
  98.1 5.0 %convert_reduce_fusion.2 = (f32[]{:T(128)}, f32[]{:T(128)}, f32[8192]{0:T(1024)S(1)}, f32[8192]{0:T(1024)S(1)}) fusion(bf16[8192,67]{1,0:T(8,128)(2,1)S(1)} %copy-done), kind=kLoop, calls=%fused_computation.30 | loop fusion | flops 49150 | bytes 114696 | tf_op jit(solution)/shard_map/reduce_sum | solution.py:33
  103.0 49.9 %while.33 = (s32[]{:T(128)}, f32[8,128]{1,0:T(8,128)S(1)}, s32[8]{0:T(128)S(1)}, bf16[1024,128]{1,0:T(8,128)(2,1)S(1)}, bf16[8192,128]{1,0:T(8,128)(2,1)}, /*ind...) while((s32[]{:T(128)}, f32[8,128]{1,0:T(8,128)S(1)}, ...), condition=%wide.region_8.0_spmd, body=%wide.region_5.8_spmd.sunk | while | flops 276823936 | bytes 10591411 | solution.py:69
  111.9 2.8 fusion.51
  118.1 2.8 fusion.51
  124.4 2.8 fusion.51
  130.6 2.8 fusion.51
  136.8 2.8 fusion.51
  154.6 24.1 %all-reduce.1 = f32[8208]{0:T(1024)S(1)} all-reduce(f32[8208]{0:T(1024)S(1)} %dynamic-update-slice.3), channel_id=2, replica_groups=mesh['row'=32,'col'=8] {'col'}, use_global_device_ids=true, to_apply=%add.1 | all-reduce | flops 8208 | bytes 65664
  180.8 51.2 %while.34 = (s32[]{:T(128)}, f32[8,8192]{1,0:T(8,128)S(1)}, f32[8,8192]{1,0:T(8,128)S(1)}, s32[8]{0:T(128)S(1)}, bf16[1024,128]{1,0:T(8,128)(2,1)S(1)}, /*index=...) while((s32[]{:T(128)}, f32[8,8192]{1,0:T(8,128)S(1)}, ...), condition=%wide.region_17.18_spmd, body=%wide.region_14.0_spmd.sunk | while | flops 276807680 | bytes 10816703 | solution.py:86
  233.6 71.0 %all-gather.7.cloned.1.call-done = f32[262144]{0:T(1024)} async-done(((f32[8192]{0:T(1024)}), f32[262144]{0:T(1024)}) %all-gather.7.cloned.1.call-update) | async-done | bytes 1048592 | tf_op jit(solution)/shard_map/all_gather | solution.py:90
  306.9 81.9 %while.35 = (s32[]{:T(128)}, f32[8,128,129]{1,0,2:T(8,128)}, s32[8]{0:T(128)S(1)}, bf16[1024,128]{1,0:T(8,128)(2,1)S(1)}, bf16[8192,128]{1,0:T(8,128)(2,1)}, /*i...) while((s32[]{:T(128)}, f32[8,128,129]{1,0,2:T(8,128)}, ...), condition=%wide.region_25.26_spmd, body=%wide.region_23.25_spmd.sunk | while | flops 545275904 | bytes 8952507 | solution.py:101
  309.6 3.2 convert_reduce_fusion.4
  313.8 3.3 dynamic_update_slice.22
  319.8 3.2 convert_reduce_fusion.4
  324.1 3.3 dynamic_update_slice.22
  330.1 3.2 convert_reduce_fusion.4
  334.3 3.3 dynamic_update_slice.22
  340.3 3.2 convert_reduce_fusion.4
  344.6 3.3 dynamic_update_slice.22
  350.6 3.2 convert_reduce_fusion.4
  354.8 3.3 dynamic_update_slice.22
  360.8 3.2 convert_reduce_fusion.4
  365.0 3.3 dynamic_update_slice.22
  371.0 3.2 convert_reduce_fusion.4
  375.3 3.3 dynamic_update_slice.22
  381.3 3.2 convert_reduce_fusion.4
  385.5 3.3 dynamic_update_slice.22
  390.8 32.8 %reduce-scatter.2.cloned.1.call-done = f32[128,129]{0,1:T(8,128)} async-done(((f32[1024,129]{0,1:T(8,128)}), f32[128,129]{0,1:T(8,128)}) %reduce-scatter.2.cloned.1.call-update) | async-done | bytes 66064 | tf_op jit(solution)/shard_map/reduce_scatter | solution.py:102
  (209 shorter events, 89.7 us)
Async XLA Ops:
  7.2 83.5 %all-gather.5.cloned.1.call-start = ((), (), s32[]{:S(2)}) async-start(), calls=%async_computation.1 | async-start | bytes 2162688 | tf_op jit(solution)/shard_map/all_gather | solution.py:29
  11.2 293.4 %all-gather.7.cloned.1.call-start = ((), (), s32[]{:S(2)}) async-start(), calls=%async_computation.3 | async-start | bytes 1081344 | tf_op jit(solution)/shard_map/all_gather | solution.py:90
  90.7 4.0 copy-start
  232.8 190.8 %reduce-scatter.2.cloned.1.call-start = ((), (), s32[]{:S(2)}) async-start(), calls=%async_computation.2 | async-start | bytes 626688 | tf_op jit(solution)/shard_map/reduce_scatter | solution.py:102
  306.9 117.4 %copy-start.1 = (bf16[128,64]{0,1:T(8,128)(2,1)S(1)}, bf16[128,64]{0,1:T(8,128)(2,1)}, u32[]{:S(2)}) copy-start(bf16[128,64]{0,1:T(8,128)(2,1)} %param.20) | copy-start | bytes 49156
  306.9 117.4 %copy-start.2 = (bf16[128,64]{0,1:T(8,128)(2,1)S(1)}, bf16[128,64]{0,1:T(8,128)(2,1)}, u32[]{:S(2)}) copy-start(bf16[128,64]{0,1:T(8,128)(2,1)} %param.16) | copy-start | bytes 49156
  306.9 117.4 %copy-start.3 = (f32[64]{0:T(128)S(1)}, f32[64]{0:T(128)}, u32[]{:S(2)}) copy-start(f32[64]{0:T(128)} %param.23) | copy-start | bytes 772
Sparse Core Ops, SparseCore 0:
  11.3 79.3 all-gather.4
  233.0 71.5 all-gather.6
  391.0 32.6 reduce-scatter.1
where the time goes:
time: 435 us; the launch traced here: 432 us
  waiting for transfers between devices  164 us (38%)
  matrix products  77.7 us (18%)
  local copies, waits for them, and re-layouts  59.4 us (14%)
  loops' own time  46.6 us (11%)
  blocking collectives  37.7 us (9%)
  other arithmetic  30.7 us (7%)
  between operations  16 us (4%)
    all_gather x1, waiting for transfers between devices, on_device(): col_all = lax.all_gather(col_local, 'row', axis=0)  71 us
    dot_general x24, matrix products, block_z(): jnp.dot(cut(q_aug, start), y_aug.T, preferred_element_type=jnp.float32)  69.9 us
    all_gather x1, waiting for transfers between devices, on_device(): y_cols_pack = lax.all_gather(y_pack, 'row', axis=0, tiled=True)  60.3 us
    reduce_scatter x1, waiting for transfers between devices, on_device(): own = lax.psum_scatter(both, 'col', scatter_dimension=0, tiled=True)  32.8 us
    dynamic_update_slice x16, local copies, waits for them, and re-layouts, on_device(): both = lax.map(moment_pass, starts).reshape(nrows, 2 * width + 1)  27.1 us
    unnamed x1, blocking collectives  24.1 us
    another operation x1, loops' own time, on_device(): col_tops, col_totals = lax.map(col_pass, starts)  15.8 us
    another operation x1, loops' own time, on_device(): both = lax.map(moment_pass, starts).reshape(nrows, 2 * width + 1)  15.8 us
  transfers between devices with their start and end apart: 3, of which 3 were waited for; matrix products, arithmetic and copies ran while one was open for 1% of the time, Pallas kernels for 0%

commit v1 on v0

--- a/solution.py
+++ b/solution.py
@@ -26,7 +26,9 @@
     y_pack = jnp.concatenate(
         [y_points, col_potential[:, None], col_mass[:, None], own_rmass[:, None]], axis=1
     )
-    y_cols_pack = lax.all_gather(y_pack, "row", axis=0, tiled=True)
+    y_cols_pack = jnp.concatenate(
+        lax.all_to_all(jnp.stack([y_pack] * lax.axis_size("row")), "row", 0, 0), axis=0
+    )
     y_cols = y_cols_pack[:, :width]
     pot_cols = y_cols_pack[:, width].astype(jnp.float32)
     mass_cols = y_cols_pack[:, width + 1].astype(jnp.float32)

time: 435 us -> 393 us (0.903)
  waiting for transfers between devices: 164 us -> 110 us
  starting transfers between devices: 0.12 us -> 11.8 us
  other arithmetic: 30.7 us -> 20.7 us
  local copies, waits for them, and re-layouts: 59.4 us -> 66.7 us
    all_gather x1 -> x0, waiting for transfers between devices: 60.3 us -> none  [on_device(): y_cols_pack = lax.all_gather(y_pack, 'row', axis=0, tiled=True)]
    all_to_all x0 -> x1, starting transfers between devices: none -> 11.6 us  [on_device(): lax.all_to_all(jnp.stack([y_pack] * lax.axis_size('row')), 'row', 0, 0)]
    all_to_all x0 -> x1, waiting for transfers between devices: none -> 11.6 us  [on_device(): lax.all_to_all(jnp.stack([y_pack] * lax.axis_size('row')), 'row', 0, 0)]
    while x0 -> x2, local copies, waits for them, and re-layouts: none -> 5.68 us  [the longest x1 3.22 us: on_device(): both = lax.map(moment_pass, starts).reshape(nrows, 2 * width + 1)]
    all_gather x1, waiting for transfers between devices: 71 us -> 65.9 us  [on_device(): col_all = lax.all_gather(col_local, 'row', axis=0)]
  transfers between devices with their start and end apart: 3 -> 3, of which waited for: 3 -> 3; matrix products, arithmetic and copies ran while one was open for 1% -> 2% of each run, Pallas kernels for 0% -> 0%
where the time goes in v1:
time: 393 us; the launch traced here: 390 us
  waiting for transfers between devices  110 us (28%)
  matrix products  77.8 us (20%)
  local copies, waits for them, and re-layouts  66.7 us (17%)
  loops' own time  48.4 us (12%)
  blocking collectives  38.3 us (10%)
  other arithmetic  20.7 us (5%)
  between operations  16.3 us (4%)
  starting transfers between devices  11.8 us (3%)
    dot_general x24, matrix products, block_z(): jnp.dot(cut(q_aug, start), y_aug.T, preferred_element_type=jnp.float32)  70 us
    all_gather x1, waiting for transfers between devices, on_device(): col_all = lax.all_gather(col_local, 'row', axis=0)  65.9 us
    reduce_scatter x1, waiting for transfers between devices, on_device(): own = lax.psum_scatter(both, 'col', scatter_dimension=0, tiled=True)  32.7 us
    dynamic_update_slice x16, local copies, waits for them, and re-layouts, on_device(): both = lax.map(moment_pass, starts).reshape(nrows, 2 * width + 1)  27 us
    unnamed x1, blocking collectives  24.7 us
    another operation x1, loops' own time, on_device(): row_local = lax.map(row_pass, starts).reshape(nrows)  16.8 us
    another operation x1, loops' own time, on_device(): col_tops, col_totals = lax.map(col_pass, starts)  15.8 us
    another operation x1, loops' own time, on_device(): both = lax.map(moment_pass, starts).reshape(nrows, 2 * width + 1)  15.8 us
  transfers between devices with their start and end apart: 3, of which 3 were waited for; matrix products, arithmetic and copies ran while one was open for 2% of the time, Pallas kernels for 0%

profile of v1, /device:TPU:4, one launch (start us, length us, event | category | flops | bytes accessed | tf_op | source)
XLA Modules:
  0.0 390.2 jit_solution(18299831699002412679)
XLA Ops:
  10.4 11.6 %all-to-all-start = ((bf16[32,256,67]{1,2,0:T(8,128)(2,1)}), bf16[32,256,67]{1,2,0:T(8,128)(2,1)S(1)}, u32[]{:S(2)}, u32[]{:S(2)}) async-start(bf16[32,256,67]{1,2,0:T(8,128)(2,1)} %stack.6), calls=%async_computation | async-start | bytes 2359296 | tf_op jit(solution)/shard_map/all_to_all | solution.py:30
  26.5 13.6 %all_gather.13 = bf16[1024,129]{1,0:T(8,128)(2,1)S(1)} all-gather(bf16[128,129]{1,0:T(8,128)(2,1)S(1)} %pad_maximum_fusion.3), channel_id=1, replica_groups=mesh['row'=32,'col'=8] {'col'}, dimensions={0}, use_global_device_ids=true | all-gather | bytes 297216 | tf_op jit(solution)/shard_map/all_gather | solution.py:20
  41.3 11.6 %all-to-all-done = bf16[32,256,67]{1,2,0:T(8,128)(2,1)S(1)} async-done(((bf16[32,256,67]{1,2,0:T(8,128)(2,1)}), bf16[32,256,67]{1,2,0:T(8,128)(2,1)S(1)}, u32[]{:S(2)}, u32[]{:S(2)}) %all-to-all-start) | async-done | bytes 1097760 | tf_op jit(solution)/shard_map/all_to_all | solution.py:30
  59.4 52.2 %while.33 = (s32[]{:T(128)}, f32[8,128]{1,0:T(8,128)S(1)}, s32[8]{0:T(128)S(1)}, bf16[1024,128]{1,0:T(8,128)(2,1)S(1)}, bf16[8192,128]{1,0:T(8,128)(2,1)}, /*ind...) while((s32[]{:T(128)}, f32[8,128]{1,0:T(8,128)S(1)}, ...), condition=%wide.region_8.0_spmd, body=%wide.region_5.8_spmd.sunk | while | flops 276823936 | bytes 10591411 | solution.py:71
  68.9 2.8 fusion.54
  75.4 2.8 fusion.54
  81.9 2.8 fusion.54
  88.5 2.8 fusion.54
  95.0 2.8 fusion.54
  101.5 2.8 fusion.54
  113.3 24.7 %all-reduce.1 = f32[8208]{0:T(1024)S(1)} all-reduce(f32[8208]{0:T(1024)S(1)} %dynamic-update-slice.3), channel_id=2, replica_groups=mesh['row'=32,'col'=8] {'col'}, use_global_device_ids=true, to_apply=%add.1 | all-reduce | flops 8208 | bytes 65664
  140.1 51.2 %while.34 = (s32[]{:T(128)}, f32[8,8192]{1,0:T(8,128)S(1)}, f32[8,8192]{1,0:T(8,128)S(1)}, s32[8]{0:T(128)S(1)}, bf16[1024,128]{1,0:T(8,128)(2,1)S(1)}, /*index=...) while((s32[]{:T(128)}, f32[8,8192]{1,0:T(8,128)S(1)}, ...), condition=%wide.region_17.18_spmd, body=%wide.region_14.0_spmd.sunk | while | flops 276807680 | bytes 10816703 | solution.py:88
  193.1 3.2 copy.54
  196.3 65.9 %all-gather.4.cloned.1.call-done = f32[262144]{0:T(1024)} async-done(((f32[8192]{0:T(1024)}), f32[262144]{0:T(1024)}) %all-gather.4.cloned.1.call-update) | async-done | bytes 1048592 | tf_op jit(solution)/shard_map/all_gather | solution.py:92
  264.5 82.0 %while.35 = (s32[]{:T(128)}, f32[8,128,129]{1,0,2:T(8,128)}, s32[8]{0:T(128)S(1)}, bf16[1024,128]{1,0:T(8,128)(2,1)}, bf16[8192,128]{1,0:T(8,128)(2,1)}, /*index...) while((s32[]{:T(128)}, f32[8,128,129]{1,0,2:T(8,128)}, ...), condition=%wide.region_25.26_spmd, body=%wide.region_23.25_spmd.sunk | while | flops 545275904 | bytes 8952507 | solution.py:103
  267.2 3.2 convert_reduce_fusion.2
  271.5 3.3 dynamic_update_slice.22
  277.5 3.2 convert_reduce_fusion.2
  281.7 3.3 dynamic_update_slice.22
  287.7 3.2 convert_reduce_fusion.2
  292.0 3.3 dynamic_update_slice.22
  298.0 3.2 convert_reduce_fusion.2
  302.2 3.3 dynamic_update_slice.22
  308.2 3.2 convert_reduce_fusion.2
  312.5 3.3 dynamic_update_slice.22
  318.5 3.2 convert_reduce_fusion.2
  322.7 3.3 dynamic_update_slice.22
  328.7 3.2 convert_reduce_fusion.2
  333.0 3.3 dynamic_update_slice.22
  338.9 3.2 convert_reduce_fusion.2
  343.2 3.3 dynamic_update_slice.22
  348.5 32.7 %reduce-scatter.2.cloned.1.call-done = f32[128,129]{0,1:T(8,128)} async-done(((f32[1024,129]{0,1:T(8,128)}), f32[128,129]{0,1:T(8,128)}) %reduce-scatter.2.cloned.1.call-update) | async-done | bytes 66064 | tf_op jit(solution)/shard_map/reduce_scatter | solution.py:104
  (216 shorter events, 93.5 us)
Async XLA Ops:
  7.2 33.5 %copy-start.3 = (f32[64]{0:T(128)S(1)}, f32[64]{0:T(128)}, u32[]{:S(2)}) copy-start(f32[64]{0:T(128)} %param.22) | copy-start | bytes 772
  10.4 42.5 %all-to-all-start = ((bf16[32,256,67]{1,2,0:T(8,128)(2,1)}), bf16[32,256,67]{1,2,0:T(8,128)(2,1)S(1)}, u32[]{:S(2)}, u32[]{:S(2)}) async-start(bf16[32,256,67]{1,2,0:T(8,128)(2,1)} %stack.6), calls=%async_computation | async-start | bytes 2359296 | tf_op jit(solution)/shard_map/all_to_all | solution.py:30
  22.0 240.2 %all-gather.4.cloned.1.call-start = ((), (), s32[]{:S(2)}) async-start(), calls=%async_computation.3 | async-start | bytes 1081344 | tf_op jit(solution)/shard_map/all_gather | solution.py:92
  191.3 5.0 %copy-start = (bf16[1024,128]{1,0:T(8,128)(2,1)}, bf16[1024,128]{1,0:T(8,128)(2,1)S(1)}, u32[]{:S(2)}) copy-start(bf16[1024,128]{1,0:T(8,128)(2,1)S(1)} %get-tuple-element.659) | copy-start | bytes 786436
  192.1 189.1 %reduce-scatter.2.cloned.1.call-start = ((), (), s32[]{:S(2)}) async-start(), calls=%async_computation.2 | async-start | bytes 626688 | tf_op jit(solution)/shard_map/reduce_scatter | solution.py:104
  264.5 117.3 %copy-start.1 = (bf16[128,64]{0,1:T(8,128)(2,1)S(1)}, bf16[128,64]{0,1:T(8,128)(2,1)}, u32[]{:S(2)}) copy-start(bf16[128,64]{0,1:T(8,128)(2,1)} %param.20) | copy-start | bytes 49156
  264.5 117.3 %copy-start.2 = (bf16[128,64]{0,1:T(8,128)(2,1)S(1)}, bf16[128,64]{0,1:T(8,128)(2,1)}, u32[]{:S(2)}) copy-start(bf16[128,64]{0,1:T(8,128)(2,1)} %param.16) | copy-start | bytes 49156
  264.5 117.3 %copy-start.4 = (f32[64]{0:T(128)S(1)}, f32[64]{0:T(128)}, u32[]{:S(2)}) copy-start(f32[64]{0:T(128)} %param.23) | copy-start | bytes 772
Sparse Core Ops, SparseCore 0:
  192.3 69.8 all-gather.3
  348.6 32.5 reduce-scatter.1
